TPU v7x, 32 devices: a whole 2x2x4 slice. The times are simulated.
32 devices in a mesh: group: 2 (over x), seq: 8 (over z, y), dp: 2 (over core).
Axes of the slice: x: 2, y: 2, z: 4, core: 2. Of those that a mesh axis runs over, the one named last changes fastest.
Arguments:
- queries: bfloat16 [4, 1024, 512], P(('group', 'dp'), 'seq'), parts along dimension 0, may hold values from -6 to 6
- key_rows: bfloat16 [4, 1024, 512], P(('group', 'dp'), 'seq'), parts along dimension 0, may hold values from -6 to 6
- value_rows: bfloat16 [4, 1024, 768], P(('group', 'dp'), 'seq'), parts along dimension 0, may hold values from -6 to 6
- trunk_state: bfloat16 [4, 1024, 768], P(('group', 'dp'), 'seq'), parts along dimension 0, may hold values from -6 to 6
- skip_input: bfloat16 [4, 2048, 768], P(('group', 'dp'), 'seq'), parts along dimension 0, may hold values from -6 to 6
- norm_gain: bfloat16 [768], replicated, may hold values from 0.099609375 to 1.8984375
- conv_weight: bfloat16 [3840, 384], replicated, may hold values from -0.09375 to 0.09375
- cotangent: bfloat16 [4, 2048, 384], P(('group', 'dp'), 'seq'), parts along dimension 0, may hold values from -6 to 6
Outputs:
- decoded: bfloat16 [4, 2048, 384], P(('group', 'dp'), 'seq'), parts along dimension 0
- grad_queries: bfloat16 [4, 1024, 512], P(('group', 'dp'), 'seq'), parts along dimension 0
- grad_keys: bfloat16 [4, 1024, 512], P(('group', 'dp'), 'seq'), parts along dimension 0
- grad_values: bfloat16 [4, 1024, 768], P(('group', 'dp'), 'seq'), parts along dimension 0
- grad_trunk: bfloat16 [4, 1024, 768], P(('group', 'dp'), 'seq'), parts along dimension 0
- grad_skip: bfloat16 [4, 2048, 768], P(('group', 'dp'), 'seq'), parts along dimension 0
- grad_weight: float32 [7680, 384], P(('group', 'seq', 'dp')), parts along dimension 0
There are 2 independent parts, one for each index of `group`. A program takes and returns all parts, laid end to end along the dimension named above; an argument that names none is the same for every part. Nothing has to cross between parts.
All inputs are finite; a program needn't handle non-finite values.
Results may differ from a plain program's by a relative error of at most 0.029.
Values may be sent and summed in bfloat16 or wider, within the bound.
No kernel may reach another device: no remote copies, remote signals or barrier semaphores. Data moves between devices by JAX's collectives and lax.ppermute only.
A program may use at most 128 MiB of HBM per device.

v0:
```python
import math
import jax
import jax.numpy as jnp
from jax import lax
from jax.sharding import PartitionSpec as P

H = 4
DK = 128
DV = 192
C = 768
CO = 384
KW = 5


def extended(array, sides, width):
    for axis, dim in sides:
        count, length = (lax.axis_size(axis), array.shape[dim])
        up = [(i, (i + 1) % count) for i in range(count - 1)]
        down = [(j, i) for i, j in up]
        last = lax.slice_in_dim(array, length - width, length, axis=dim)
        initial = lax.slice_in_dim(array, 0, width, axis=dim)
        before = lax.ppermute(last, axis, up)
        after = lax.ppermute(initial, axis, down)
        array = jnp.concatenate([before, array, after], axis=dim)
    return array


def gelu_parts(preact):
    cdf_value = 0.5 * (1.0 + jax.scipy.special.erf(preact * (1.0 / math.sqrt(2.0))))
    density = jnp.exp(-0.5 * preact * preact) * (1.0 / math.sqrt(2.0 * math.pi))
    return (preact * cdf_value, cdf_value + preact * density)


def window_rows(padded, kernel, row_count):
    return jnp.concatenate(
        [padded[offset : offset + row_count] for offset in range(kernel)], axis=1
    )


def body(queries, key_rows, value_rows, trunk_state, skip_input, norm_gain, conv_weight, cotangent):
    score_scale = DK ** (-0.5)
    local_tokens = queries.shape[1]
    positions = 2 * local_tokens
    half_kernel = KW // 2
    query_heads = queries[0].reshape(local_tokens, H, DK)
    gathered = (
        lax.all_gather(key_rows, "seq", axis=1, tiled=True),
        lax.all_gather(value_rows, "seq", axis=1, tiled=True),
    )
    all_keys = gathered[0][0].reshape(-1, H, DK)
    all_values = gathered[1][0].reshape(-1, H, DV)
    scores = (
        jnp.einsum("ihd,jhd->hij", query_heads, all_keys, preferred_element_type=jnp.float32)
        * score_scale
    )
    row_peak = jnp.max(scores, axis=2, keepdims=True)
    row_total = jnp.sum(jnp.exp(scores - row_peak), axis=2, keepdims=True)
    logsum = row_peak + jnp.log(row_total)
    softmax = jnp.exp(scores - logsum)
    rounded = softmax.astype(jnp.bfloat16)
    attended = jnp.einsum(
        "hij,jhd->ihd", rounded, all_values, preferred_element_type=jnp.float32
    ).astype(jnp.bfloat16)
    hidden = trunk_state[0].astype(jnp.float32) + attended.reshape(local_tokens, H * DV).astype(
        jnp.float32
    )
    merged = jnp.repeat(hidden, 2, axis=0) + skip_input[0].astype(jnp.float32)
    inverse = lax.rsqrt(jnp.mean(merged * merged, axis=1, keepdims=True) + 1e-06)
    channel_gain = norm_gain.astype(jnp.float32)
    normed = (merged * inverse * channel_gain).astype(jnp.bfloat16)
    padded = extended(normed, (("seq", 0),), half_kernel)
    columns = window_rows(padded, KW, positions)
    preact = jnp.dot(columns, conv_weight, preferred_element_type=jnp.float32)
    activated, derivative = gelu_parts(preact)
    decoded = activated.astype(jnp.bfloat16)
    grad_pre = (cotangent[0].astype(jnp.float32) * derivative).astype(jnp.bfloat16)
    grad_padded = extended(grad_pre, (("seq", 0),), half_kernel)
    norm_scale = (lax.axis_size("dp") * positions * lax.axis_size("seq")) ** (-0.5)
    grad_weight = lax.psum_scatter(
        lax.dot_general(
            columns, grad_pre, (((0,), (0,)), ((), ())), preferred_element_type=jnp.float32
        )
        * norm_scale,
        ("seq", "dp"),
        scatter_dimension=0,
        tiled=True,
    )
    stacked = jnp.stack(
        [
            grad_padded[2 * half_kernel - offset : 2 * half_kernel - offset + positions]
            for offset in range(KW)
        ],
        axis=1,
    )
    weight_blocks = conv_weight.reshape(KW, C, CO)
    grad_normed = jnp.einsum(
        "pko,kco->pc", stacked, weight_blocks, preferred_element_type=jnp.float32
    )
    scaled_grad = grad_normed * channel_gain
    grad_merged = inverse * scaled_grad - merged * inverse**3 * jnp.mean(
        scaled_grad * merged, axis=1, keepdims=True
    )
    grad_skip = grad_merged.astype(jnp.bfloat16)
    grad_trunk = grad_merged.reshape(local_tokens, 2, C).sum(axis=1).astype(jnp.bfloat16)
    grad_heads = grad_trunk.reshape(local_tokens, H, DV)
    row_delta = jnp.sum(grad_heads.astype(jnp.float32) * attended.astype(jnp.float32), axis=2)
    value_grad = jnp.einsum(
        "ihd,jhd->hij", grad_heads, all_values, preferred_element_type=jnp.float32
    )
    slopes = (softmax * (value_grad - row_delta.T[:, :, None])).astype(jnp.bfloat16)
    grad_queries = (
        jnp.einsum("hij,jhd->ihd", slopes, all_keys, preferred_element_type=jnp.float32)
        * score_scale
    ).astype(jnp.bfloat16)
    key_part = (
        jnp.einsum("hij,ihd->jhd", slopes, query_heads, preferred_element_type=jnp.float32)
        * score_scale
    )
    value_part = jnp.einsum("hij,ihd->jhd", rounded, grad_heads, preferred_element_type=jnp.float32)
    summed = lax.psum_scatter(
        jnp.concatenate(
            [
                key_part.reshape(lax.axis_size("seq") * local_tokens, H * DK),
                value_part.reshape(lax.axis_size("seq") * local_tokens, H * DV),
            ],
            axis=1,
        ).astype(jnp.bfloat16),
        "seq",
        scatter_dimension=0,
        tiled=True,
    ).astype(jnp.float32)
    grad_keys = summed[:, : H * DK].astype(jnp.bfloat16)
    grad_values = summed[:, H * DK :].astype(jnp.bfloat16)
    return (
        decoded[None],
        grad_queries.reshape(local_tokens, H * DK)[None],
        grad_keys[None],
        grad_values[None],
        grad_trunk[None],
        grad_skip[None],
        grad_weight,
    )


def solution(mesh):
    return jax.shard_map(
        body,
        mesh=mesh,
        in_specs=(
            P(("group", "dp"), "seq", None),
            P(("group", "dp"), "seq", None),
            P(("group", "dp"), "seq", None),
            P(("group", "dp"), "seq", None),
            P(("group", "dp"), "seq", None),
            P(),
            P(),
            P(("group", "dp"), "seq", None),
        ),
        out_specs=(
            P(("group", "dp"), "seq", None),
            P(("group", "dp"), "seq", None),
            P(("group", "dp"), "seq", None),
            P(("group", "dp"), "seq", None),
            P(("group", "dp"), "seq", None),
            P(("group", "dp"), "seq", None),
            P(("group", "seq", "dp"), None),
        ),
        check_vma=False,
    )
```

profile of v0, /device:TPU:0, one launch (start us, length us, event | category | flops | bytes accessed | tf_op | source)
XLA Modules:
  0.0 324.4 jit_solution(8928119127070148307)
XLA Ops:
  7.2 0.0 copy-start
  7.2 0.0 all-gather.3.cloned.1.call-start
  7.2 1.8 copy.24
  9.0 0.0 all-gather.3.cloned.1.call-update
  9.1 0.0 all-gather.5.cloned.1.call-start
  9.1 0.7 all-gather.5.cloned.1.call-update
  9.8 0.0 reduce-scatter.3.cloned.1.call-start
  9.9 0.7 convert_element_type.100
  10.6 1.0 copy.35
  11.6 0.0 copy-start.11
  11.6 41.2 %all-gather.3.cloned.1.call-done = bf16[1,1024,512]{1,2,0:T(8,128)(2,1)} async-done(((bf16[1,128,512]{1,2,0:T(8,128)(2,1)}), bf16[1,1024,512]{1,2,0:T(8,128)(2,1)}) %all-gather.3.cloned.1.call-update) | async-done | bytes 1048592 | tf_op jit(solution)/shard_map/all_gather | solution.py:47
  52.8 1.8 multiply_reduce_fusion
  54.6 1.3 copy-done.1
  55.9 0.5 exponential_reduce_fusion
  56.4 41.8 %all-gather.5.cloned.1.call-done = bf16[1,1024,768]{2,1,0:T(8,128)(2,1)} async-done(((bf16[1,128,768]{2,1,0:T(8,128)(2,1)}), bf16[1,1024,768]{2,1,0:T(8,128)(2,1)}) %all-gather.5.cloned.1.call-update) | async-done | bytes 1572880 | tf_op jit(solution)/shard_map/all_gather | solution.py:48
  98.2 2.6 copy.27
  100.8 2.8 fusion.2
  103.5 0.9 copy.28
  104.5 1.0 convert_add_fusion.1
  105.5 1.2 broadcast_in_dim.12
  106.7 2.6 reshape.93
  109.2 2.6 broadcast_in_dim.26
  111.8 1.3 fusion.6
  113.2 1.3 multiply_convert_fusion.2
  114.4 0.0 copy-start.14
  114.5 2.6 collective-permute-start
  117.1 1.3 collective-permute-start.1
  118.4 0.1 fusion.10
  118.5 0.1 fusion.18
  118.6 4.3 %collective-permute-done.1 = bf16[2,768]{1,0:T(2,128)(2,1)S(1)} collective-permute-done((bf16[2,768]{1,0:T(2,128)(2,1)S(1)}, bf16[2,768]{1,0:T(2,128)(2,1)S(1)}, u32[]{:S(2)}, u32[]{:S(2)}) %collective-permute-start.1) | collective-permute-done | bytes 3104 | tf_op jit(solution)/shard_map/ppermute | solution.py:23
  122.9 0.1 fusion.8
  123.0 0.1 fusion.17
  123.1 2.0 fusion.16
  125.2 1.4 collective-permute-start.2
  126.6 5.4 %collective-permute-start.3 = (bf16[2,384]{1,0:T(2,128)(2,1)S(1)}, bf16[2,384]{1,0:T(2,128)(2,1)S(1)}, u32[]{:S(2)}, u32[]{:S(2)}) collective-permute-start(bf16[2,384]{1,0:T(2,128)(2,1)S(1)} %get-tuple-element.27), channel_id=1, source_target_pairs={{0,2},{2,4},{4,6},{6,8},{8,10},{10,12},{12,14},{1,3},{3,5},{5,7},{... | collective-permute-start | bytes 4616 | tf_op jit(solution)/shard_map/ppermute | solution.py:22
  132.1 0.1 fusion.25
  132.1 0.1 fusion.30
  132.2 1.1 collective-permute-done.3
  133.3 0.1 fusion.22
  133.4 0.1 fusion.28
  133.5 1.1 multiply_reduce_fusion.1
  134.6 1.3 convert_bitcast_fusion.1
  135.9 2.5 reshape.95
  138.4 2.8 reduce_sum.48
  141.2 1.7 copy.29
  142.9 1.1 fusion.19
  144.1 3.6 %convolution_convert_fusion = bf16[4,192,1024]{2,1,0:T(8,128)(2,1)} fusion(bf16[128,4,192]{0,2,1:T(8,128)(2,1)} %bitcast.94, f32[4,128,1024]{2,1,0:T(8,128)} %copy-done.1, f32[4,128]{1,0:T(4,128)S(1)} %log_add_fusion), kind=kOutput, calls=%fused_computation.8 | convolution fusion | flops 203685888 | bytes 3868672 | tf_op jit(solution)/shard_map/hij,ihd->jhd/dot_general | solution.py:119
  147.7 0.0 copy-start.12
  147.7 0.8 multiply_convert_fusion.1
  148.6 1.0 copy-done.5
  149.6 1.4 multiply_convert_fusion
  151.0 2.3 copy.31
  153.2 2.6 copy.32
  155.9 3.4 %pad_maximum_fusion = bf16[1024,1280]{1,0:T(8,128)(2,1)} fusion(bf16[1024,768]{1,0:T(8,128)(2,1)} %copy.32, bf16[1024,512]{1,0:T(8,128)(2,1)} %copy.31), kind=kLoop, calls=%fused_computation.1 | loop fusion | flops 5242880 | bytes 5242880 | tf_op jit(solution)/shard_map/concatenate | solution.py:121
  159.3 0.0 reduce-scatter.3.cloned.1.call-update
  159.3 0.0 reduce-scatter.5.cloned.1.call-start
  159.3 5.3 %convolution_multiply_fusion = f32[3840,384]{1,0:T(8,128)} fusion(bf16[256,3840]{1,0:T(8,128)(2,1)} %copy-done.7, bf16[256,384]{1,0:T(8,128)(2,1)S(1)} %get-tuple-element.23), kind=kOutput, calls=%fused_computation | convolution fusion | flops 756449280 | bytes 8060928 | tf_op jit(solution)/shard_map/dot_general | solution.py:80
  164.6 0.0 reduce-scatter.5.cloned.1.call-update
  164.7 2.0 fusion.3
  166.6 0.8 copy.33
  167.4 64.6 %reduce-scatter.3.cloned.1.call-done = bf16[128,1280]{1,0:T(8,128)(2,1)} async-done(((bf16[1024,1280]{1,0:T(8,128)(2,1)}), bf16[128,1280]{1,0:T(8,128)(2,1)}) %reduce-scatter.3.cloned.1.call-update) | async-done | bytes 327696 | tf_op jit(solution)/shard_map/reduce_scatter | solution.py:120
  232.0 1.6 slice_bitcast_fusion.1
  233.6 1.6 slice_bitcast_fusion
  235.2 82.7 %reduce-scatter.5.cloned.1.call-done = f32[240,384]{1,0:T(8,128)} async-done(((f32[3840,384]{1,0:T(8,128)}), f32[240,384]{1,0:T(8,128)}) %reduce-scatter.5.cloned.1.call-update) | async-done | bytes 368656 | tf_op jit(solution)/shard_map/reduce_scatter | solution.py:79
  (33 shorter events, 0.2 us)
Async XLA Ops:
  7.2 115.9 %copy-start = (bf16[3840,384]{1,0:T(8,128)(2,1)S(1)}, bf16[3840,384]{1,0:T(8,128)(2,1)}, u32[]{:S(2)}) copy-start(bf16[3840,384]{1,0:T(8,128)(2,1)} %param.14) | copy-start | bytes 8847364
  7.2 45.6 %all-gather.3.cloned.1.call-start = ((), (), s32[]{:S(2)}) async-start(), calls=%async_computation.2 | async-start | bytes 1179648 | tf_op jit(solution)/shard_map/all_gather | solution.py:47
  9.1 89.1 %all-gather.5.cloned.1.call-start = ((), (), s32[]{:S(2)}) async-start(), calls=%async_computation.3 | async-start | bytes 1769472 | tf_op jit(solution)/shard_map/all_gather | solution.py:48
  9.8 222.2 %reduce-scatter.3.cloned.1.call-start = ((), (), s32[]{:S(2)}) async-start(), calls=%async_computation.4 | async-start | bytes 2949120 | tf_op jit(solution)/shard_map/reduce_scatter | solution.py:120
  11.6 44.8 %copy-start.11 = (bf16[1,128,512]{1,2,0:T(8,128)(2,1)}, bf16[1,128,512]{1,2,0:T(8,128)(2,1)S(1)}, u32[]{:S(2)}) copy-start(bf16[1,128,512]{1,2,0:T(8,128)(2,1)S(1)} %copy.35) | copy-start | bytes 393220
  54.5 1.3 copy-start.1
  100.8 3.7 %copy-start.13 = (bf16[1,128,768]{2,1,0:T(8,128)(2,1)S(1)}, bf16[1,128,768]{2,1,0:T(8,128)(2,1)}, u32[]{:S(2)}) copy-start(bf16[1,128,768]{2,1,0:T(8,128)(2,1)} %param.11) | copy-start | bytes 589828
  103.5 0.9 copy-start.8
  105.5 6.3 %copy-start.6 = (bf16[1,256,768]{2,1,0:T(8,128)(2,1)S(1)}, bf16[1,256,768]{2,1,0:T(8,128)(2,1)}, u32[]{:S(2)}) copy-start(bf16[1,256,768]{2,1,0:T(8,128)(2,1)} %param.12) | copy-start | bytes 1179652
  114.4 8.7 %copy-start.14 = (bf16[1,256,384]{2,1,0:T(8,128)(2,1)S(1)}, bf16[1,256,384]{2,1,0:T(8,128)(2,1)}, u32[]{:S(2)}) copy-start(bf16[1,256,384]{2,1,0:T(8,128)(2,1)} %param.15) | copy-start | bytes 589828
  114.5 3.9 %collective-permute-start = (bf16[2,768]{1,0:T(2,128)(2,1)S(1)}, bf16[2,768]{1,0:T(2,128)(2,1)S(1)}, u32[]{:S(2)}, u32[]{:S(2)}) collective-permute-start(bf16[2,768]{1,0:T(2,128)(2,1)S(1)} %get-tuple-element.26), channel_id=1, source_target_pairs={{0,2},{2,4},{4,6},{6,8},{8,10},{10,12},{12,14},{1,3},{3,5},{5,7},{... | collective-permute-start | bytes 9224 | tf_op jit(solution)/shard_map/ppermute | solution.py:22
  117.1 5.8 %collective-permute-start.1 = (bf16[2,768]{1,0:T(2,128)(2,1)S(1)}, bf16[2,768]{1,0:T(2,128)(2,1)S(1)}, u32[]{:S(2)}, u32[]{:S(2)}) collective-permute-start(bf16[2,768]{1,0:T(2,128)(2,1)S(1)} %get-tuple-element.25), channel_id=1, source_target_pairs={{2,0},{4,2},{6,4},{8,6},{10,8},{12,10},{14,12},{3,1},{5,3},{7,5},{... | collective-permute-start | bytes 9224 | tf_op jit(solution)/shard_map/ppermute | solution.py:23
  123.1 2.0 copy-start.7
  125.1 8.3 %copy-start.4 = (f32[256,768]{1,0:T(8,128)S(1)}, f32[256,768]{1,0:T(8,128)}, u32[]{:S(2)}) copy-start(f32[256,768]{1,0:T(8,128)} %reshape.93) | copy-start | bytes 2359300
  125.2 6.9 %collective-permute-start.2 = (bf16[2,384]{1,0:T(2,128)(2,1)S(1)}, bf16[2,384]{1,0:T(2,128)(2,1)S(1)}, u32[]{:S(2)}, u32[]{:S(2)}) collective-permute-start(bf16[2,384]{1,0:T(2,128)(2,1)S(1)} %get-tuple-element.28), channel_id=1, source_target_pairs={{2,0},{4,2},{6,4},{8,6},{10,8},{12,10},{14,12},{3,1},{5,3},{7,5},{... | collective-permute-start | bytes 4616 | tf_op jit(solution)/shard_map/ppermute | solution.py:23
  126.6 6.7 %collective-permute-start.3 = (bf16[2,384]{1,0:T(2,128)(2,1)S(1)}, bf16[2,384]{1,0:T(2,128)(2,1)S(1)}, u32[]{:S(2)}, u32[]{:S(2)}) collective-permute-start(bf16[2,384]{1,0:T(2,128)(2,1)S(1)} %get-tuple-element.27), channel_id=1, source_target_pairs={{0,2},{2,4},{4,6},{6,8},{8,10},{10,12},{12,14},{1,3},{3,5},{5,7},{... | collective-permute-start | bytes 4616 | tf_op jit(solution)/shard_map/ppermute | solution.py:22
  135.9 7.0 %copy-start.9 = (f32[4,128,192]{1,2,0:T(8,128)S(1)}, f32[4,128,192]{1,2,0:T(8,128)}, u32[]{:S(2)}) copy-start(f32[4,128,192]{1,2,0:T(8,128)} %copy-done.8) | copy-start | bytes 1179652
  142.9 4.8 %copy-start.2 = (f32[4,128,1024]{2,1,0:T(8,128)S(1)}, f32[4,128,1024]{2,1,0:T(8,128)}, u32[]{:S(2)}) copy-start(f32[4,128,1024]{2,1,0:T(8,128)} %copy-done.1) | copy-start | bytes 6291460
  142.9 4.8 %copy-start.3 = (bf16[1,1024,768]{1,2,0:T(8,128)(2,1)S(1)}, bf16[1,1024,768]{1,2,0:T(8,128)(2,1)}, u32[]{:S(2)}) copy-start(bf16[1,1024,768]{1,2,0:T(8,128)(2,1)} %copy.27) | copy-start | bytes 4718596
  142.9 4.8 %copy-start.10 = (bf16[128,768]{0,1:T(8,128)(2,1)S(1)}, bf16[128,768]{0,1:T(8,128)(2,1)}, u32[]{:S(2)}) copy-start(bf16[128,768]{0,1:T(8,128)(2,1)} %copy.29) | copy-start | bytes 589828
  147.7 1.9 copy-start.12
  148.6 1.0 copy-start.5
  159.3 158.6 %reduce-scatter.5.cloned.1.call-start = ((), (), s32[]{:S(2)}) async-start(), calls=%async_computation.5 | async-start | bytes 6266880 | tf_op jit(solution)/shard_map/reduce_scatter | solution.py:79
Sparse Core Ops, SparseCore 0:
  10.6 42.1 all-gather.2
  54.9 43.1 all-gather.4
  159.4 72.5 reduce-scatter.2
  236.4 81.4 reduce-scatter.4
where the time goes:
time: 325 us; the launch traced here: 324 us
  waiting for transfers between devices  236 us (73%)
  local copies, waits for them, and re-layouts  28.3 us (9%)
  matrix products  20.8 us (6%)
  other arithmetic  14 us (4%)
  between operations  14 us (4%)
  starting transfers between devices  10.9 us (3%)
    reduce_scatter x1, waiting for transfers between devices, body(): lax.psum_scatter(lax.dot_general(columns, grad_pre, (((0,), (0,)), ((), (...  82.7 us
    reduce_scatter x1, waiting for transfers between devices, body(): lax.psum_scatter(jnp.concatenate([key_part.reshape(lax.axis_size('seq') *...  64.6 us
    all_gather x1, waiting for transfers between devices, body(): lax.all_gather(value_rows, 'seq', axis=1, tiled=True)  41.8 us
    all_gather x1, waiting for transfers between devices, body(): lax.all_gather(key_rows, 'seq', axis=1, tiled=True)  41.2 us
    ppermute x2, starting transfers between devices, extended(): before = lax.ppermute(last, axis, up)  8.03 us
  transfers between devices with their start and end apart: 8, of which 6 were waited for; matrix products, arithmetic and copies ran while one was open for 5% of the time, Pallas kernels for 0%

commit v1 on v0

--- a/solution.py
+++ b/solution.py
@@ -1,3 +1,4 @@
+import functools
 import math
 import jax
 import jax.numpy as jnp
@@ -10,6 +11,41 @@
 C = 768
 CO = 384
 KW = 5
+
+
+def wait_links(patch, device_axis):
+    d_next, y_new, p_next = (
+        lax.axis_size(device_axis),
+        lax.axis_index(device_axis),
+        patch.shape[1],
+    )
+    line_up = tuple((c * d_next if to_i == 1 else c for to_i, c in enumerate(patch.shape)))
+    a_now = lax.dynamic_update_slice_in_dim(
+        jnp.zeros(line_up, patch.dtype), patch, y_new * p_next, axis=1
+    )
+    mid_arr = formed = patch
+    for idx in range(1, d_next // 2 + 1):
+        mid_arr = lax.ppermute(
+            mid_arr,
+            axis_name=device_axis,
+            perm=tuple(((to_i, (to_i + 1) % d_next) for to_i in range(d_next))),
+        )
+        a_now = lax.dynamic_update_slice_in_dim(
+            a_now, mid_arr, (y_new - idx) % d_next * p_next, axis=1
+        )
+        if 2 * idx < d_next:
+            formed = lax.ppermute(
+                formed,
+                axis_name=device_axis,
+                perm=tuple(((to_i, (to_i - 1) % d_next) for to_i in range(d_next))),
+            )
+            a_now = lax.dynamic_update_slice_in_dim(
+                a_now, formed, (y_new + idx) % d_next * p_next, axis=1
+            )
+    return a_now
+
+
+do_packet = functools.partial(wait_links, device_axis="seq")
 
 
 def extended(array, sides, width):
@@ -43,10 +79,7 @@
     positions = 2 * local_tokens
     half_kernel = KW // 2
     query_heads = queries[0].reshape(local_tokens, H, DK)
-    gathered = (
-        lax.all_gather(key_rows, "seq", axis=1, tiled=True),
-        lax.all_gather(value_rows, "seq", axis=1, tiled=True),
-    )
+    gathered = (lax.all_gather(key_rows, "seq", axis=1, tiled=True), do_packet(value_rows))
     all_keys = gathered[0][0].reshape(-1, H, DK)
     all_values = gathered[1][0].reshape(-1, H, DV)
     scores = (

time: 325 us -> 289 us (0.89)
  waiting for transfers between devices: 236 us -> 171 us
  starting transfers between devices: 10.9 us -> 26.4 us
  local copies, waits for them, and re-layouts: 28.3 us -> 40.2 us
    all_gather x1 -> x0, waiting for transfers between devices: 41.8 us -> none  [body(): lax.all_gather(value_rows, 'seq', axis=1, tiled=True)]
    all_gather x1, waiting for transfers between devices: 41.2 us -> 0.01 us  [body(): lax.all_gather(key_rows, 'seq', axis=1, tiled=True)]
    ppermute x0 -> x7, waiting for transfers between devices: none -> 20.3 us  [the longest x4 16.6 us: wait_links(): lax.ppermute(mid_arr, axis_name=device_axis, perm=tuple(((to_i, (to_i + 1...]
    ppermute x0 -> x7, starting transfers between devices: none -> 17.4 us  [the longest x3 16.1 us: wait_links(): lax.ppermute(formed, axis_name=device_axis, perm=tuple(((to_i, (to_i - 1)...]
    ppermute x0 -> x7, local copies, waits for them, and re-layouts: none -> 7.61 us  [the longest x4 4.34 us: wait_links(): lax.ppermute(mid_arr, axis_name=device_axis, perm=tuple(((to_i, (to_i + 1...]
    dynamic_update_slice x0 -> x8, local copies, waits for them, and re-layouts: none -> 5.78 us  [the longest x4 2.91 us: wait_links(): lax.dynamic_update_slice_in_dim(a_now, mid_arr, (y_new - idx) % d_next *...]
  transfers between devices with their start and end apart: 8 -> 14, of which waited for: 6 -> 7; matrix products, arithmetic and copies ran while one was open for 5% -> 10% of each run, Pallas kernels for 0% -> 0%
where the time goes in v1:
time: 289 us; the launch traced here: 288 us
  waiting for transfers between devices  171 us (59%)
  local copies, waits for them, and re-layouts  40.2 us (14%)
  starting transfers between devices  26.4 us (9%)
  matrix products  21.8 us (8%)
  between operations  14.1 us (5%)
  other arithmetic  14 us (5%)
    reduce_scatter x1, waiting for transfers between devices, body(): lax.psum_scatter(lax.dot_general(columns, grad_pre, (((0,), (0,)), ((), (...  82.8 us
    reduce_scatter x1, waiting for transfers between devices, body(): lax.psum_scatter(jnp.concatenate([key_part.reshape(lax.axis_size('seq') *...  63 us
    ppermute x4, waiting for transfers between devices, wait_links(): lax.ppermute(mid_arr, axis_name=device_axis, perm=tuple(((to_i, (to_i + 1...  16.6 us
    ppermute x3, starting transfers between devices, wait_links(): lax.ppermute(formed, axis_name=device_axis, perm=tuple(((to_i, (to_i - 1)...  16.1 us
    ppermute x2, starting transfers between devices, extended(): before = lax.ppermute(last, axis, up)  6.15 us
  transfers between devices with their start and end apart: 14, of which 7 were waited for; matrix products, arithmetic and copies ran while one was open for 10% of the time, Pallas kernels for 0%

profile of v1, /device:TPU:0, one launch (start us, length us, event | category | flops | bytes accessed | tf_op | source)
XLA Modules:
  0.0 287.5 jit_solution(3637251710829692601)
XLA Ops:
  7.2 1.8 copy.39
  9.1 6.1 %collective-permute-start.1 = (bf16[1,128,768]{2,1,0:T(8,128)(2,1)}, bf16[1,128,768]{2,1,0:T(8,128)(2,1)}, u32[]{:S(2)}, u32[]{:S(2)}) collective-permute-start(bf16[1,128,768]{2,1,0:T(8,128)(2,1)} %param.10), channel_id=1, source_target_pairs={{0,14},{2,0},{4,2},{6,4},{8,6},{10,8},{12,10},{14,12},{1,15},{3,1}... | collective-permute-start | bytes 589832 | tf_op jit(solution)/shard_map/ppermute | solution.py:37
  15.2 1.2 copy.31
  16.4 0.7 convert_element_type.100
  17.0 1.0 copy.49
  18.1 1.4 broadcast_in_dim.28
  19.5 0.7 constant_dynamic-update-slice_fusion.8
  20.2 1.1 copy.33
  21.3 4.8 %collective-permute-start.3 = (bf16[1,128,768]{2,1,0:T(8,128)(2,1)}, bf16[1,128,768]{2,1,0:T(8,128)(2,1)}, u32[]{:S(2)}, u32[]{:S(2)}) collective-permute-start(bf16[1,128,768]{2,1,0:T(8,128)(2,1)} %collective-permute-done.1), channel_id=1, source_target_pairs={{0,14},{2,0},{4,2},{6,4},{8,6},{10,8},{12,10},{14,12},{1,15},{3,1}... | collective-permute-start | bytes 589832 | tf_op jit(solution)/shard_map/ppermute | solution.py:37
  26.1 1.1 copy.32
  27.3 0.7 constant_dynamic-update-slice_fusion.7
  28.0 0.7 constant_dynamic-update-slice_fusion.6
  28.7 3.6 %collective-permute-done.3 = bf16[1,128,768]{2,1,0:T(8,128)(2,1)} collective-permute-done((bf16[1,128,768]{2,1,0:T(8,128)(2,1)}, bf16[1,128,768]{2,1,0:T(8,128)(2,1)}, u32[]{:S(2)}, u32[]{:S(2)}) %collective-permute-start.3) | collective-permute-done | bytes 196640 | tf_op jit(solution)/shard_map/ppermute | solution.py:37
  32.4 1.1 copy.35
  33.4 5.2 %collective-permute-start.5 = (bf16[1,128,768]{2,1,0:T(8,128)(2,1)}, bf16[1,128,768]{2,1,0:T(8,128)(2,1)}, u32[]{:S(2)}, u32[]{:S(2)}) collective-permute-start(bf16[1,128,768]{2,1,0:T(8,128)(2,1)} %collective-permute-done.3), channel_id=1, source_target_pairs={{0,14},{2,0},{4,2},{6,4},{8,6},{10,8},{12,10},{14,12},{1,15},{3,1}... | collective-permute-start | bytes 589832 | tf_op jit(solution)/shard_map/ppermute | solution.py:37
  38.7 1.1 copy.34
  39.8 0.7 constant_dynamic-update-slice_fusion.5
  40.5 0.7 constant_dynamic-update-slice_fusion.4
  41.3 8.8 %collective-permute-done.4 = bf16[1,128,768]{2,1,0:T(8,128)(2,1)} collective-permute-done((bf16[1,128,768]{2,1,0:T(8,128)(2,1)}, bf16[1,128,768]{2,1,0:T(8,128)(2,1)}, u32[]{:S(2)}, u32[]{:S(2)}) %collective-permute-start.4) | collective-permute-done | bytes 196640 | tf_op jit(solution)/shard_map/ppermute | solution.py:28
  50.0 1.1 copy.36
  51.1 1.1 collective-permute-start.6
  52.3 1.1 copy.37
  53.4 0.8 constant_dynamic-update-slice_fusion.3
  54.1 0.7 constant_dynamic-update-slice_fusion.2
  54.8 7.8 %collective-permute-done.6 = bf16[1,128,768]{2,1,0:T(8,128)(2,1)} collective-permute-done((bf16[1,128,768]{2,1,0:T(8,128)(2,1)}, bf16[1,128,768]{2,1,0:T(8,128)(2,1)}, u32[]{:S(2)}, u32[]{:S(2)}) %collective-permute-start.6) | collective-permute-done | bytes 196640 | tf_op jit(solution)/shard_map/ppermute | solution.py:28
  62.7 1.1 copy.38
  63.8 0.7 constant_dynamic-update-slice_fusion.1
  64.5 1.8 multiply_reduce_fusion
  66.3 0.5 exponential_reduce_fusion
  66.8 2.4 fusion.2
  69.2 0.9 copy.42
  70.1 1.0 convert_add_fusion.1
  71.2 1.1 broadcast_in_dim.29
  72.3 2.6 reshape.93
  74.9 2.6 broadcast_in_dim.30
  77.5 1.3 fusion.6
  78.8 1.3 multiply_convert_fusion.2
  80.1 1.4 collective-permute-start.7
  81.6 1.3 collective-permute-start.8
  83.1 3.9 %collective-permute-done.8 = bf16[2,768]{1,0:T(2,128)(2,1)S(1)} collective-permute-done((bf16[2,768]{1,0:T(2,128)(2,1)S(1)}, bf16[2,768]{1,0:T(2,128)(2,1)S(1)}, u32[]{:S(2)}, u32[]{:S(2)}) %collective-permute-start.8) | collective-permute-done | bytes 3104 | tf_op jit(solution)/shard_map/ppermute | solution.py:59
  87.3 2.0 fusion.16
  89.3 1.4 collective-permute-start.9
  90.7 4.7 %collective-permute-start.10 = (bf16[2,384]{1,0:T(2,128)(2,1)S(1)}, bf16[2,384]{1,0:T(2,128)(2,1)S(1)}, u32[]{:S(2)}, u32[]{:S(2)}) collective-permute-start(bf16[2,384]{1,0:T(2,128)(2,1)S(1)} %get-tuple-element.27), channel_id=1, source_target_pairs={{0,2},{2,4},{4,6},{6,8},{8,10},{10,12},{12,14},{1,3},{3,5},{5,7},{... | collective-permute-start | bytes 4616 | tf_op jit(solution)/shard_map/ppermute | solution.py:58
  95.6 0.9 collective-permute-done.10
  96.7 1.1 multiply_reduce_fusion.1
  97.8 1.3 convert_bitcast_fusion.1
  99.1 2.5 reshape.95
  101.6 2.8 reduce_sum.48
  104.4 1.7 copy.43
  106.1 1.1 fusion.19
  107.3 3.5 %convolution_convert_fusion = bf16[4,192,1024]{2,1,0:T(8,128)(2,1)} fusion(bf16[128,4,192]{0,2,1:T(8,128)(2,1)} %bitcast.92, f32[4,128,1024]{2,1,0:T(8,128)} %copy-done.1, f32[4,128]{1,0:T(4,128)S(1)} %log_add_fusion), kind=kOutput, calls=%fused_computation.8 | convolution fusion | flops 203685888 | bytes 3868672 | tf_op jit(solution)/shard_map/hij,ihd->jhd/dot_general | solution.py:152
  110.8 2.3 multiply_convert_fusion.1
  113.1 1.0 copy-done.4
  114.1 1.4 multiply_convert_fusion
  115.5 2.3 copy.45
  117.8 2.6 copy.46
  120.4 3.4 %pad_maximum_fusion = bf16[1024,1280]{1,0:T(8,128)(2,1)} fusion(bf16[1024,768]{1,0:T(8,128)(2,1)} %copy.46, bf16[1024,512]{1,0:T(8,128)(2,1)} %copy.45), kind=kLoop, calls=%fused_computation.1 | loop fusion | flops 5242880 | bytes 5242880 | tf_op jit(solution)/shard_map/concatenate | solution.py:154
  123.9 5.3 %convolution_multiply_fusion = f32[3840,384]{1,0:T(8,128)} fusion(bf16[256,3840]{1,0:T(8,128)(2,1)} %copy-done.6, bf16[256,384]{1,0:T(8,128)(2,1)S(1)} %get-tuple-element.23), kind=kOutput, calls=%fused_computation | convolution fusion | flops 756449280 | bytes 8060928 | tf_op jit(solution)/shard_map/dot_general | solution.py:113
  129.2 2.0 fusion.3
  131.2 0.8 copy.47
  131.9 63.0 %reduce-scatter.3.cloned.1.call-done = bf16[128,1280]{1,0:T(8,128)(2,1)} async-done(((bf16[1024,1280]{1,0:T(8,128)(2,1)}), bf16[128,1280]{1,0:T(8,128)(2,1)}) %reduce-scatter.3.cloned.1.call-update) | async-done | bytes 327696 | tf_op jit(solution)/shard_map/reduce_scatter | solution.py:153
  195.0 1.6 slice_bitcast_fusion.1
  196.5 1.6 slice_bitcast_fusion
  198.2 82.8 %reduce-scatter.5.cloned.1.call-done = f32[240,384]{1,0:T(8,128)} async-done(((f32[3840,384]{1,0:T(8,128)}), f32[240,384]{1,0:T(8,128)}) %reduce-scatter.5.cloned.1.call-update) | async-done | bytes 368656 | tf_op jit(solution)/shard_map/reduce_scatter | solution.py:112
  (58 shorter events, 1.1 us)
Async XLA Ops:
  7.2 80.1 %copy-start = (bf16[3840,384]{1,0:T(8,128)(2,1)S(1)}, bf16[3840,384]{1,0:T(8,128)(2,1)}, u32[]{:S(2)}) copy-start(bf16[3840,384]{1,0:T(8,128)(2,1)} %param.14) | copy-start | bytes 8847364
  7.2 57.3 %all-gather.2.cloned.1.call-start = ((), (), s32[]{:S(2)}) async-start(), calls=%async_computation.2 | async-start | bytes 1179648 | tf_op jit(solution)/shard_map/all_gather | solution.py:82
  9.1 185.9 %reduce-scatter.3.cloned.1.call-start = ((), (), s32[]{:S(2)}) async-start(), calls=%async_computation.3 | async-start | bytes 2949120 | tf_op jit(solution)/shard_map/reduce_scatter | solution.py:153
  9.1 11.1 %collective-permute-start.1 = (bf16[1,128,768]{2,1,0:T(8,128)(2,1)}, bf16[1,128,768]{2,1,0:T(8,128)(2,1)}, u32[]{:S(2)}, u32[]{:S(2)}) collective-permute-start(bf16[1,128,768]{2,1,0:T(8,128)(2,1)} %param.10), channel_id=1, source_target_pairs={{0,14},{2,0},{4,2},{6,4},{8,6},{10,8},{12,10},{14,12},{1,15},{3,1}... | collective-permute-start | bytes 589832 | tf_op jit(solution)/shard_map/ppermute | solution.py:37
  15.2 10.9 %collective-permute-start = (bf16[1,128,768]{2,1,0:T(8,128)(2,1)}, bf16[1,128,768]{2,1,0:T(8,128)(2,1)}, u32[]{:S(2)}, u32[]{:S(2)}) collective-permute-start(bf16[1,128,768]{2,1,0:T(8,128)(2,1)} %param.10), channel_id=1, source_target_pairs={{0,2},{2,4},{4,6},{6,8},{8,10},{10,12},{12,14},{14,0},{1,3},{3,5},... | collective-permute-start | bytes 589832 | tf_op jit(solution)/shard_map/ppermute | solution.py:28
  18.1 46.4 %copy-start.10 = (bf16[1,128,512]{1,2,0:T(8,128)(2,1)}, bf16[1,128,512]{1,2,0:T(8,128)(2,1)S(1)}, u32[]{:S(2)}) copy-start(bf16[1,128,512]{1,2,0:T(8,128)(2,1)S(1)} %copy.49) | copy-start | bytes 393220
  21.3 11.0 %collective-permute-start.3 = (bf16[1,128,768]{2,1,0:T(8,128)(2,1)}, bf16[1,128,768]{2,1,0:T(8,128)(2,1)}, u32[]{:S(2)}, u32[]{:S(2)}) collective-permute-start(bf16[1,128,768]{2,1,0:T(8,128)(2,1)} %collective-permute-done.1), channel_id=1, source_target_pairs={{0,14},{2,0},{4,2},{6,4},{8,6},{10,8},{12,10},{14,12},{1,15},{3,1}... | collective-permute-start | bytes 589832 | tf_op jit(solution)/shard_map/ppermute | solution.py:37
  27.2 11.5 %collective-permute-start.2 = (bf16[1,128,768]{2,1,0:T(8,128)(2,1)}, bf16[1,128,768]{2,1,0:T(8,128)(2,1)}, u32[]{:S(2)}, u32[]{:S(2)}) collective-permute-start(bf16[1,128,768]{2,1,0:T(8,128)(2,1)} %collective-permute-done), channel_id=1, source_target_pairs={{0,2},{2,4},{4,6},{6,8},{8,10},{10,12},{12,14},{14,0},{1,3},{3,5},... | collective-permute-start | bytes 589832 | tf_op jit(solution)/shard_map/ppermute | solution.py:28
  33.4 18.8 %collective-permute-start.5 = (bf16[1,128,768]{2,1,0:T(8,128)(2,1)}, bf16[1,128,768]{2,1,0:T(8,128)(2,1)}, u32[]{:S(2)}, u32[]{:S(2)}) collective-permute-start(bf16[1,128,768]{2,1,0:T(8,128)(2,1)} %collective-permute-done.3), channel_id=1, source_target_pairs={{0,14},{2,0},{4,2},{6,4},{8,6},{10,8},{12,10},{14,12},{1,15},{3,1}... | collective-permute-start | bytes 589832 | tf_op jit(solution)/shard_map/ppermute | solution.py:37
  39.8 10.3 %collective-permute-start.4 = (bf16[1,128,768]{2,1,0:T(8,128)(2,1)}, bf16[1,128,768]{2,1,0:T(8,128)(2,1)}, u32[]{:S(2)}, u32[]{:S(2)}) collective-permute-start(bf16[1,128,768]{2,1,0:T(8,128)(2,1)} %collective-permute-done.2), channel_id=1, source_target_pairs={{0,2},{2,4},{4,6},{6,8},{8,10},{10,12},{12,14},{14,0},{1,3},{3,5},... | collective-permute-start | bytes 589832 | tf_op jit(solution)/shard_map/ppermute | solution.py:28
  51.1 11.5 %collective-permute-start.6 = (bf16[1,128,768]{2,1,0:T(8,128)(2,1)}, bf16[1,128,768]{2,1,0:T(8,128)(2,1)}, u32[]{:S(2)}, u32[]{:S(2)}) collective-permute-start(bf16[1,128,768]{2,1,0:T(8,128)(2,1)} %collective-permute-done.4), channel_id=1, source_target_pairs={{0,2},{2,4},{4,6},{6,8},{8,10},{10,12},{12,14},{14,0},{1,3},{3,5},... | collective-permute-start | bytes 589832 | tf_op jit(solution)/shard_map/ppermute | solution.py:28
  66.3 2.9 %copy-start.1 = (f32[4,128,1024]{2,1,0:T(8,128)}, f32[4,128,1024]{2,1,0:T(8,128)S(1)}, u32[]{:S(2)}) copy-start(f32[4,128,1024]{2,1,0:T(8,128)S(1)} %get-tuple-element.32) | copy-start | bytes 6291460
  66.8 3.3 %copy-start.12 = (bf16[1,128,768]{2,1,0:T(8,128)(2,1)S(1)}, bf16[1,128,768]{2,1,0:T(8,128)(2,1)}, u32[]{:S(2)}) copy-start(bf16[1,128,768]{2,1,0:T(8,128)(2,1)} %param.11) | copy-start | bytes 589828
  69.2 0.9 copy-start.7
  71.2 6.3 %copy-start.5 = (bf16[1,256,768]{2,1,0:T(8,128)(2,1)S(1)}, bf16[1,256,768]{2,1,0:T(8,128)(2,1)}, u32[]{:S(2)}) copy-start(bf16[1,256,768]{2,1,0:T(8,128)(2,1)} %param.12) | copy-start | bytes 1179652
  80.1 7.2 %copy-start.13 = (bf16[1,256,384]{2,1,0:T(8,128)(2,1)S(1)}, bf16[1,256,384]{2,1,0:T(8,128)(2,1)}, u32[]{:S(2)}) copy-start(bf16[1,256,384]{2,1,0:T(8,128)(2,1)} %param.15) | copy-start | bytes 589828
  80.1 2.7 collective-permute-start.7
  81.6 5.5 %collective-permute-start.8 = (bf16[2,768]{1,0:T(2,128)(2,1)S(1)}, bf16[2,768]{1,0:T(2,128)(2,1)S(1)}, u32[]{:S(2)}, u32[]{:S(2)}) collective-permute-start(bf16[2,768]{1,0:T(2,128)(2,1)S(1)} %get-tuple-element.25), channel_id=1, source_target_pairs={{2,0},{4,2},{6,4},{8,6},{10,8},{12,10},{14,12},{3,1},{5,3},{7,5},{... | collective-permute-start | bytes 9224 | tf_op jit(solution)/shard_map/ppermute | solution.py:59
  87.3 2.0 copy-start.6
  89.3 7.4 %copy-start.3 = (f32[256,768]{1,0:T(8,128)S(1)}, f32[256,768]{1,0:T(8,128)}, u32[]{:S(2)}) copy-start(f32[256,768]{1,0:T(8,128)} %reshape.93) | copy-start | bytes 2359300
  89.3 6.2 %collective-permute-start.9 = (bf16[2,384]{1,0:T(2,128)(2,1)S(1)}, bf16[2,384]{1,0:T(2,128)(2,1)S(1)}, u32[]{:S(2)}, u32[]{:S(2)}) collective-permute-start(bf16[2,384]{1,0:T(2,128)(2,1)S(1)} %get-tuple-element.28), channel_id=1, source_target_pairs={{2,0},{4,2},{6,4},{8,6},{10,8},{12,10},{14,12},{3,1},{5,3},{7,5},{... | collective-permute-start | bytes 4616 | tf_op jit(solution)/shard_map/ppermute | solution.py:59
  90.7 5.8 %collective-permute-start.10 = (bf16[2,384]{1,0:T(2,128)(2,1)S(1)}, bf16[2,384]{1,0:T(2,128)(2,1)S(1)}, u32[]{:S(2)}, u32[]{:S(2)}) collective-permute-start(bf16[2,384]{1,0:T(2,128)(2,1)S(1)} %get-tuple-element.27), channel_id=1, source_target_pairs={{0,2},{2,4},{4,6},{6,8},{8,10},{10,12},{12,14},{1,3},{3,5},{5,7},{... | collective-permute-start | bytes 4616 | tf_op jit(solution)/shard_map/ppermute | solution.py:58
  99.1 7.0 %copy-start.8 = (f32[4,192,128]{2,1,0:T(8,128)S(1)}, f32[4,192,128]{2,1,0:T(8,128)}, u32[]{:S(2)}) copy-start(f32[4,192,128]{2,1,0:T(8,128)} %copy-done.7) | copy-start | bytes 1179652
  106.1 4.7 %copy-start.2 = (f32[4,128,1024]{2,1,0:T(8,128)S(1)}, f32[4,128,1024]{2,1,0:T(8,128)}, u32[]{:S(2)}) copy-start(f32[4,128,1024]{2,1,0:T(8,128)} %copy-done.1) | copy-start | bytes 6291460
  106.1 4.7 %copy-start.9 = (bf16[128,768]{0,1:T(8,128)(2,1)S(1)}, bf16[128,768]{0,1:T(8,128)(2,1)}, u32[]{:S(2)}) copy-start(bf16[128,768]{0,1:T(8,128)(2,1)} %copy.43) | copy-start | bytes 589828
  110.8 3.3 %copy-start.11 = (bf16[1,128,512]{1,2,0:T(8,128)(2,1)S(1)}, bf16[1,128,512]{1,2,0:T(8,128)(2,1)}, u32[]{:S(2)}) copy-start(bf16[1,128,512]{1,2,0:T(8,128)(2,1)} %copy-done.10) | copy-start | bytes 393220
  113.1 1.0 copy-start.4
  123.8 157.2 %reduce-scatter.5.cloned.1.call-start = ((), (), s32[]{:S(2)}) async-start(), calls=%async_computation.4 | async-start | bytes 6266880 | tf_op jit(solution)/shard_map/reduce_scatter | solution.py:112
Sparse Core Ops, SparseCore 0:
  10.6 45.2 all-gather.1
  123.9 70.9 reduce-scatter.2
  199.5 81.4 reduce-scatter.4
